TPU v7x, 512 devices: a whole 4x8x8 slice. The times are simulated.
512 devices in a mesh: seq: 64 (over y, x, z_hi), head: 8 (over z_lo, core).
Axes of the slice: x: 4, y: 8, z: 8 (z_hi: 2, z_lo: 4; z = z_hi * 4 + z_lo), core: 2. Of those that a mesh axis runs over, the one named last changes fastest.
Arguments:
- queries: bfloat16 [32768, 16, 128], P('seq', 'head'), may hold values from -6 to 6
- keys: bfloat16 [32768, 16, 128], P('seq', 'head'), may hold values from -6 to 6
- values: bfloat16 [32768, 16, 128], P('seq', 'head'), may hold values from -6 to 6
- clusters: int32 [16, 32768, 1], P('head', 'seq'), may hold values from 0 to 255; in each aligned block of 512 rows (0 to 511, 512 to 1023, ..., all dimensions but the last counted through in order) at most 8 rows name the same one
- cent_keys: bfloat16 [16, 256, 128], P('head', 'seq'), may hold values from -6 to 6
- cent_values: bfloat16 [16, 256, 128], P('head', 'seq'), may hold values from -6 to 6
- out_weight: bfloat16 [2048, 4096], P('head'), may hold values from -0.1875 to 0.1875
Outputs:
- mixed: bfloat16 [4096, 32768], P('head', 'seq')
Inputs may be any that keep to these rules, and one draw needn't show every extreme that they name: `clusters`: among the 512 tokens of one device in one head (an aligned block of rows), no cluster is named more than 8 times; in some such block a cluster is named exactly 8 times.
All inputs are finite; a program needn't handle non-finite values.
Results may differ from a plain program's by a relative error of at most 0.017.
Values may be sent and summed in bfloat16 or wider, within the bound.
No kernel may reach another device: no remote copies, remote signals or barrier semaphores. Data moves between devices by JAX's collectives and lax.ppermute only.
A program may use at most 128 MiB of HBM per device.

v0:
```python
import jax
import jax.numpy as jnp
from jax import lax
from jax.sharding import PartitionSpec as P

CLUSTERS = 256
MOST = 8


def masked_scores(query_in, key_in, where_in, scale):
    sources, count, depth, width = query_in.shape
    nheads = where_in.shape[3]
    hsize = width // nheads
    query_five = query_in.reshape(sources, count, depth, nheads, hsize)
    key_five = key_in.reshape(sources, count, depth, nheads, hsize)
    raw = jnp.einsum(
        "aimhe,bikhe->ihambk", query_five, key_five, preferred_element_type=jnp.float32
    )
    scores = raw.reshape(count, nheads, sources * depth, sources * depth) * scale
    where_now = jnp.transpose(where_in, (1, 3, 0, 2)).reshape(count, nheads, sources * depth)
    allowed = (where_now[:, :, None, :] >= 0) & (
        where_now[:, :, None, :] <= where_now[:, :, :, None]
    )
    return (jnp.where(allowed, scores, -1e30), query_five)


def weigh_values(rounded, value_in):
    sources, count, depth, width = value_in.shape
    nheads = rounded.shape[1]
    value_five = value_in.reshape(sources, count, depth, nheads, width // nheads)
    shaped = rounded.reshape(count, nheads, sources * depth, sources, depth)
    return jnp.einsum("ihqbk,bikhe->ihqe", shaped, value_five, preferred_element_type=jnp.float32)


def to_slots(array_in, sources, depth):
    count, nheads = (array_in.shape[0], array_in.shape[1])
    tail = array_in.shape[3:]
    shaped = array_in.reshape((count, nheads, sources, depth) + tail)
    if len(tail) == 1:
        moved = jnp.transpose(shaped, (2, 0, 3, 1, 4))
        return moved.reshape(sources, count, depth, nheads * tail[0])
    return jnp.transpose(shaped, (2, 0, 3, 1))


def on_device(queries, keys, values, clusters, cent_keys, cent_values, out_weight):
    tok_dev, heads_dev, head_dim = queries.shape
    owners = lax.axis_size("seq")
    per_owner = CLUSTERS // owners
    slot_total = CLUSTERS * MOST
    scale = head_dim ** (-0.5)
    assign = clusters[:, :, 0]
    order = jnp.arange(tok_dev, dtype=jnp.int32)
    earlier = (assign[:, :, None] == assign[:, None, :]) & (
        order[None, None, :] < order[None, :, None]
    )
    rank = jnp.sum(earlier.astype(jnp.int32), axis=2)
    slot_of = (assign * MOST + rank).T
    head_cols = jnp.arange(heads_dev, dtype=jnp.int32)[None, :]
    position = lax.axis_index("seq") * tok_dev + order

    def place(rows_in):
        empty = jnp.zeros((slot_total, heads_dev, head_dim), rows_in.dtype)
        filled = empty.at[slot_of, head_cols].set(rows_in)
        return filled.reshape(owners, per_owner, MOST, heads_dev * head_dim)

    where_buf = jnp.full((slot_total, heads_dev), -1, jnp.int32)
    where_buf = where_buf.at[slot_of, head_cols].set(
        jnp.broadcast_to(position[:, None], (tok_dev, heads_dev))
    )
    where_buf = where_buf.reshape(owners, per_owner, MOST, heads_dev)
    cent_all_k, cent_all_v = (
        lax.all_gather(cent_keys, "seq", axis=1, tiled=True),
        lax.all_gather(cent_values, "seq", axis=1, tiled=True),
    )
    query_in = lax.all_to_all(place(queries), "seq", split_axis=0, concat_axis=0, tiled=True)
    key_in = lax.all_to_all(place(keys), "seq", split_axis=0, concat_axis=0, tiled=True)
    value_in = lax.all_to_all(place(values), "seq", split_axis=0, concat_axis=0, tiled=True)
    where_in = lax.all_to_all(where_buf, "seq", split_axis=0, concat_axis=0, tiled=True)
    sources, count, depth, width = query_in.shape
    local, query_five = masked_scores(query_in, key_in, where_in, scale)
    top = jnp.max(local, axis=-1, keepdims=True)
    w_local = jnp.exp(local - top)
    numer = weigh_values(w_local.astype(jnp.bfloat16), value_in)
    denom = jnp.sum(w_local, axis=-1)
    returned = (
        lax.all_to_all(
            to_slots(numer, sources, depth).astype(jnp.bfloat16),
            "seq",
            split_axis=0,
            concat_axis=0,
            tiled=True,
        ).astype(jnp.float32),
        lax.all_to_all(
            to_slots(top[..., 0], sources, depth).astype(jnp.bfloat16),
            "seq",
            split_axis=0,
            concat_axis=0,
            tiled=True,
        ).astype(jnp.float32),
        lax.all_to_all(
            to_slots(denom, sources, depth).astype(jnp.bfloat16),
            "seq",
            split_axis=0,
            concat_axis=0,
            tiled=True,
        ).astype(jnp.float32),
    )
    numer_s, top_s, denom_s = returned
    numer_t = numer_s.reshape(slot_total, heads_dev, head_dim)[slot_of, head_cols]
    top_t = top_s.reshape(slot_total, heads_dev)[slot_of, head_cols]
    denom_t = denom_s.reshape(slot_total, heads_dev)[slot_of, head_cols]
    memory = (
        jnp.einsum("the,hce->thc", queries, cent_all_k, preferred_element_type=jnp.float32) * scale
    )
    top = jnp.maximum(top_t, jnp.max(memory, axis=-1))
    w_memory = jnp.exp(memory - top[:, :, None])
    factor = jnp.exp(top_t - top)
    numer = numer_t * factor[:, :, None] + jnp.einsum(
        "thc,hce->the",
        w_memory.astype(jnp.bfloat16),
        cent_all_v,
        preferred_element_type=jnp.float32,
    )
    denom = denom_t * factor + jnp.sum(w_memory, axis=-1)
    attended = (numer / denom[:, :, None]).astype(jnp.bfloat16)
    flat_out = attended.reshape(tok_dev, heads_dev * head_dim)
    return lax.psum_scatter(
        jnp.einsum("kc,tk->ct", out_weight, flat_out, preferred_element_type=jnp.float32).astype(
            jnp.bfloat16
        ),
        "head",
        scatter_dimension=0,
        tiled=True,
    )


def solution(mesh):
    return jax.shard_map(
        on_device,
        mesh=mesh,
        in_specs=(
            P("seq", "head", None),
            P("seq", "head", None),
            P("seq", "head", None),
            P("head", "seq", None),
            P("head", "seq", None),
            P("head", "seq", None),
            P("head", None),
        ),
        out_specs=P("head", "seq"),
        check_vma=False,
    )
```

profile of v0, /device:TPU:2, one launch (start us, length us, event | category | flops | bytes accessed | tf_op | source)
XLA Modules:
  0.0 806.8 jit_solution(5865518857260931860)
XLA Ops:
  6.6 0.8 copy.192
  7.4 0.7 convert_reduce_fusion
  8.2 0.7 shift-left_or_fusion
  8.9 0.7 and_reduce_fusion
  9.6 0.8 multiply_reduce_fusion.1
  10.4 0.1 copy.123
  10.5 0.2 reshape.185
  10.9 0.2 reshape.187
  11.0 4.3 scatter_custom_fusion
  15.4 0.4 reshape.128
  15.7 0.7 copy.124
  16.5 19.1 %all-to-all-start = ((s32[64,4,8,2]{2,1,3,0:T(4,128)}), s32[64,4,8,2]{2,1,3,0:T(4,128)S(1)}, u32[]{:S(2)}, u32[]{:S(2)}) async-start(s32[64,4,8,2]{2,1,3,0:T(4,128)} %copy.124), calls=%async_computation | async-start | bytes 524288 | tf_op jit(solution)/shard_map/all_to_all | solution.py:78
  35.6 0.1 copy.127
  35.7 0.2 reshape.191
  35.9 3.9 scatter_custom_fusion.1
  39.8 1.2 reshape.129
  41.0 10.4 %all-to-all-done = s32[64,4,8,2]{2,1,3,0:T(4,128)S(1)} async-done(((s32[64,4,8,2]{2,1,3,0:T(4,128)}), s32[64,4,8,2]{2,1,3,0:T(4,128)S(1)}, u32[]{:S(2)}, u32[]{:S(2)}) %all-to-all-start) | async-done | bytes 16416 | tf_op jit(solution)/shard_map/all_to_all | solution.py:78
  51.5 6.4 all-to-all-start.1
  57.9 3.9 scatter_custom_fusion.2
  61.8 1.2 reshape.131
  63.0 25.8 %all-to-all-done.1 = bf16[64,4,8,256]{3,2,1,0:T(8,128)(2,1)} async-done(((bf16[64,4,8,256]{3,2,1,0:T(8,128)(2,1)}), bf16[64,4,8,256]{3,2,1,0:T(8,128)(2,1)}, u32[]{:S(2)}, u32[]{:S(2)}) %all-to-all-start.1) | async-done | bytes 1048608 | tf_op jit(solution)/shard_map/all_to_all | solution.py:75
  88.8 7.1 all-to-all-start.2
  95.9 4.1 scatter_custom_fusion.3
  99.9 1.2 reshape.133
  101.2 0.2 le.25
  101.5 24.8 %all-to-all-done.2 = bf16[64,4,8,256]{3,2,1,0:T(8,128)(2,1)} async-done(((bf16[64,4,8,256]{3,2,1,0:T(8,128)(2,1)}), bf16[64,4,8,256]{3,2,1,0:T(8,128)(2,1)}, u32[]{:S(2)}, u32[]{:S(2)}) %all-to-all-start.2) | async-done | bytes 1048608 | tf_op jit(solution)/shard_map/all_to_all | solution.py:76
  126.3 7.2 all-to-all-start.3
  133.5 6.9 fusion
  140.4 5.7 copy-done.1
  146.1 6.4 exponential_reduce_fusion
  152.6 0.2 sub.34
  152.8 9.4 %copy.130 = f32[4,2,64,8,64,8]{4,5,3,2,1,0:T(8,128)S(1)} copy(f32[4,2,64,8,64,8]{4,3,5,2,1,0:T(8,128)} %copy-done.1) | data formatting | bytes 16777216 | tf_op jit(solution)/shard_map/mul | solution.py:19
  162.2 0.8 copy.148
  162.9 12.5 %exponential_convert_fusion = bf16[4,2,512,64,8]{3,4,2,1,0:T(8,128)(2,1)} fusion(f32[4,2,512,64,8]{3,4,2,1,0:T(8,128)S(1)} %bitcast.84, f32[4,2,512]{2,1,0:T(2,128)S(1)} %sub.34, s32[4,2,512]{2,1,0:T(2,128)S(1)} %le.25, s32[4,2,64,8]{2,3,1,0:T(8,128)S(1)} %bitcast.91, pred[4,2,64,8]{2,3,1,0:T(8,128)(4,1)S(1)} %broadcast_compare_fusion), kind=kLoop, calls=%fused_computation.8 | loop fusion | flops 10485760 | bytes 12636160 | tf_op jit(solution)/shard_map/convert_element_type | solution.py:83
  175.4 15.1 %all-to-all-start.6 = ((bf16[64,4,8,2]{2,1,3,0:T(4,128)(2,1)}), bf16[64,4,8,2]{2,1,3,0:T(4,128)(2,1)S(1)}, u32[]{:S(2)}, u32[]{:S(2)}) async-start(bf16[64,4,8,2]{2,1,3,0:T(4,128)(2,1)} %copy.148), calls=%async_computation.6 | async-start | bytes 262144 | tf_op jit(solution)/shard_map/all_to_all | solution.py:100
  190.6 0.8 copy.136
  191.3 12.0 %copy.132 = bf16[4,2,512,64,8]{2,4,3,1,0:T(8,128)(2,1)} copy(bf16[4,2,512,64,8]{3,4,2,1,0:T(8,128)(2,1)} %exponential_convert_fusion) | data formatting | bytes 8388608 | tf_op jit(solution)/shard_map/convert_element_type | solution.py:83
  203.3 1.2 all-to-all-done.6
  204.5 13.9 %all-to-all-start.5 = ((bf16[64,4,8,2]{2,1,3,0:T(4,128)(2,1)}), bf16[64,4,8,2]{2,1,3,0:T(4,128)(2,1)S(1)}, u32[]{:S(2)}, u32[]{:S(2)}) async-start(bf16[64,4,8,2]{2,1,3,0:T(4,128)(2,1)} %copy.136), calls=%async_computation.5 | async-start | bytes 262144 | tf_op jit(solution)/shard_map/all_to_all | solution.py:93
  218.5 4.0 fusion.2
  222.5 1.3 copy.190
  223.8 8.5 %all-to-all-done.5 = bf16[64,4,8,2]{2,1,3,0:T(4,128)(2,1)S(1)} async-done(((bf16[64,4,8,2]{2,1,3,0:T(4,128)(2,1)}), bf16[64,4,8,2]{2,1,3,0:T(4,128)(2,1)S(1)}, u32[]{:S(2)}, u32[]{:S(2)}) %all-to-all-start.5) | async-done | bytes 8224 | tf_op jit(solution)/shard_map/all_to_all | solution.py:93
  232.3 6.8 all-to-all-start.4
  239.1 0.1 copy.135
  239.3 0.2 reshape.167
  239.5 224.9 %all_gather.6 = bf16[2,256,128]{2,0,1:T(2,128)(2,1)S(1)} all-gather(bf16[2,4,128]{2,0,1:T(2,128)(2,1)S(1)} %copy.139), channel_id=1, replica_groups=mesh['seq'=64,'head'=8] {'seq'}, dimensions={1}, use_global_device_ids=true | all-gather | bytes 133120 | tf_op jit(solution)/shard_map/all_gather | solution.py:72
  464.4 227.6 %all_gather.7 = bf16[2,256,128]{2,0,1:T(2,128)(2,1)} all-gather(bf16[2,4,128]{2,0,1:T(2,128)(2,1)S(1)} %copy.145), channel_id=1, replica_groups=mesh['seq'=64,'head'=8] {'seq'}, dimensions={1}, use_global_device_ids=true | all-gather | bytes 133120 | tf_op jit(solution)/shard_map/all_gather | solution.py:73
  692.0 1.9 fusion.27
  694.2 0.3 reshape.166
  694.5 9.1 %gather_fusion.2 = f32[1024]{0:T(1024)S(1)} fusion(f32[2048,2]{0,1:T(2,128)S(1)} %reshape.166, s32[1024]{0:T(1024)S(1)} %reshape.167), kind=kCustom, calls=%fused_computation.2 | custom fusion | bytes 16384 | tf_op jit(solution)/shard_map/gather | solution.py:111
  703.6 0.2 reshape.182
  703.9 0.1 copy.137
  704.0 0.1 copy.138
  704.1 0.3 reshape.164
  704.4 9.1 %gather_fusion.1 = f32[1024]{0:T(1024)S(1)} fusion(f32[2048,2]{0,1:T(2,128)S(1)} %reshape.164, s32[1024]{0:T(1024)S(1)} %reshape.167), kind=kCustom, calls=%fused_computation.1 | custom fusion | bytes 16384 | tf_op jit(solution)/shard_map/gather | solution.py:110
  713.5 0.2 reshape.176
  713.9 0.2 fusion.10
  714.1 3.1 reshape.162
  717.2 16.2 %gather_fusion = f32[1024,128]{1,0:T(8,128)} fusion(f32[2048,2,128]{2,1,0:T(2,128)} %reshape.162, s32[1024]{0:T(1024)S(1)} %reshape.167), kind=kCustom, calls=%fused_computation | custom fusion | bytes 1056768 | tf_op jit(solution)/shard_map/gather | solution.py:109
  733.4 2.0 copy.144
  735.4 1.4 fusion.6
  736.9 3.2 fusion.1
  740.1 57.8 %reduce-scatter.2.cloned.1.call-done = bf16[512,512]{0,1:T(8,128)(2,1)} async-done(((bf16[4096,512]{0,1:T(8,128)(2,1)}), bf16[512,512]{0,1:T(8,128)(2,1)}) %reduce-scatter.2.cloned.1.call-update) | async-done | bytes 524304 | tf_op jit(solution)/shard_map/reduce_scatter | solution.py:127
  797.9 2.0 copy.152
  (35 shorter events, 1.0 us)
Async XLA Ops:
  6.5 730.3 %copy-start = (bf16[256,4096]{1,0:T(8,128)(2,1)S(1)}, bf16[256,4096]{1,0:T(8,128)(2,1)}, u32[]{:S(2)}) copy-start(bf16[256,4096]{1,0:T(8,128)(2,1)} %param.13) | copy-start | bytes 6291460
  16.5 35.0 %all-to-all-start = ((s32[64,4,8,2]{2,1,3,0:T(4,128)}), s32[64,4,8,2]{2,1,3,0:T(4,128)S(1)}, u32[]{:S(2)}, u32[]{:S(2)}) async-start(s32[64,4,8,2]{2,1,3,0:T(4,128)} %copy.124), calls=%async_computation | async-start | bytes 524288 | tf_op jit(solution)/shard_map/all_to_all | solution.py:78
  51.5 37.3 %all-to-all-start.1 = ((bf16[64,4,8,256]{3,2,1,0:T(8,128)(2,1)}), bf16[64,4,8,256]{3,2,1,0:T(8,128)(2,1)}, u32[]{:S(2)}, u32[]{:S(2)}) async-start(bf16[64,4,8,256]{3,2,1,0:T(8,128)(2,1)} %reshape.129), calls=%async_computation.1 | async-start | bytes 2097152 | tf_op jit(solution)/shard_map/all_to_all | solution.py:75
  88.8 37.5 %all-to-all-start.2 = ((bf16[64,4,8,256]{3,2,1,0:T(8,128)(2,1)}), bf16[64,4,8,256]{3,2,1,0:T(8,128)(2,1)}, u32[]{:S(2)}, u32[]{:S(2)}) async-start(bf16[64,4,8,256]{3,2,1,0:T(8,128)(2,1)} %reshape.131), calls=%async_computation.2 | async-start | bytes 2097152 | tf_op jit(solution)/shard_map/all_to_all | solution.py:76
  126.3 49.1 %all-to-all-start.3 = ((bf16[64,4,8,256]{3,2,1,0:T(8,128)(2,1)}), bf16[64,4,8,256]{3,2,1,0:T(8,128)(2,1)}, u32[]{:S(2)}, u32[]{:S(2)}) async-start(bf16[64,4,8,256]{3,2,1,0:T(8,128)(2,1)} %reshape.133), calls=%async_computation.3 | async-start | bytes 2097152 | tf_op jit(solution)/shard_map/all_to_all | solution.py:77
  140.4 5.7 copy-start.1
  175.4 29.1 %all-to-all-start.6 = ((bf16[64,4,8,2]{2,1,3,0:T(4,128)(2,1)}), bf16[64,4,8,2]{2,1,3,0:T(4,128)(2,1)S(1)}, u32[]{:S(2)}, u32[]{:S(2)}) async-start(bf16[64,4,8,2]{2,1,3,0:T(4,128)(2,1)} %copy.148), calls=%async_computation.6 | async-start | bytes 262144 | tf_op jit(solution)/shard_map/all_to_all | solution.py:100
  204.5 27.8 %all-to-all-start.5 = ((bf16[64,4,8,2]{2,1,3,0:T(4,128)(2,1)}), bf16[64,4,8,2]{2,1,3,0:T(4,128)(2,1)S(1)}, u32[]{:S(2)}, u32[]{:S(2)}) async-start(bf16[64,4,8,2]{2,1,3,0:T(4,128)(2,1)} %copy.136), calls=%async_computation.5 | async-start | bytes 262144 | tf_op jit(solution)/shard_map/all_to_all | solution.py:93
  218.5 21.0 %copy-start.5 = (bf16[2,4,128]{2,1,0:T(4,128)(2,1)S(1)}, bf16[2,4,128]{2,1,0:T(4,128)(2,1)}, u32[]{:S(2)}) copy-start(bf16[2,4,128]{2,1,0:T(4,128)(2,1)} %param.11) | copy-start | bytes 6148
  218.5 21.0 %copy-start.6 = (bf16[2,4,128]{2,1,0:T(4,128)(2,1)S(1)}, bf16[2,4,128]{2,1,0:T(4,128)(2,1)}, u32[]{:S(2)}) copy-start(bf16[2,4,128]{2,1,0:T(4,128)(2,1)} %param.12) | copy-start | bytes 6148
  218.5 473.5 %copy-start.3 = (bf16[512,2,128]{2,1,0:T(2,128)(2,1)S(1)}, bf16[512,2,128]{2,1,0:T(2,128)(2,1)}, u32[]{:S(2)}) copy-start(bf16[512,2,128]{2,1,0:T(2,128)(2,1)} %param.7) | copy-start | bytes 786436
  232.3 481.8 %all-to-all-start.4 = ((bf16[64,4,8,256]{3,2,1,0:T(8,128)(2,1)}), bf16[64,4,8,256]{3,2,1,0:T(8,128)(2,1)}, u32[]{:S(2)}, u32[]{:S(2)}) async-start(bf16[64,4,8,256]{3,2,1,0:T(8,128)(2,1)} %bitcast.81), calls=%async_computation.4 | async-start | bytes 2097152 | tf_op jit(solution)/shard_map/all_to_all | solution.py:86
  239.1 558.8 %reduce-scatter.2.cloned.1.call-start = ((), (), s32[]{:S(2)}) async-start(), calls=%async_computation.8 | async-start | bytes 4718592 | tf_op jit(solution)/shard_map/reduce_scatter | solution.py:127
  704.4 9.4 %copy-start.4 = (f32[512,2]{0,1:T(2,128)S(1)}, f32[512,2]{0,1:T(2,128)}, u32[]{:S(2)}) copy-start(f32[512,2]{0,1:T(2,128)} %get-tuple-element.15) | copy-start | bytes 12292
  704.4 9.4 %copy-start.2 = (f32[512,2,256]{0,2,1:T(8,128)S(1)}, f32[512,2,256]{0,2,1:T(8,128)}, u32[]{:S(2)}) copy-start(f32[512,2,256]{0,2,1:T(8,128)} %get-tuple-element.16) | copy-start | bytes 3145732
Sparse Core Ops, SparseCore 0:
  740.3 57.6 reduce-scatter.1
where the time goes:
time: 808 us; the launch traced here: 807 us
  blocking collectives  453 us (56%)
  waiting for transfers between devices  129 us (16%)
  local copies, waits for them, and re-layouts  96.7 us (12%)
  starting transfers between devices  75.7 us (9%)
  other arithmetic  22.2 us (3%)
  matrix products  17.4 us (2%)
  between operations  13.8 us (2%)
    all_gather x1, blocking collectives, on_device(): lax.all_gather(cent_values, 'seq', axis=1, tiled=True)  228 us
    all_gather x1, blocking collectives, on_device(): lax.all_gather(cent_keys, 'seq', axis=1, tiled=True)  225 us
    reduce_scatter x1, waiting for transfers between devices, on_device(): lax.psum_scatter(jnp.einsum('kc,tk->ct', out_weight, flat_out, preferred_...  57.8 us
    all_to_all x1, waiting for transfers between devices, on_device(): lax.all_to_all(place(queries), 'seq', split_axis=0, concat_axis=0, tiled=...  25.8 us
    all_to_all x1, waiting for transfers between devices, on_device(): lax.all_to_all(place(keys), 'seq', split_axis=0, concat_axis=0, tiled=True)  24.8 us
    unnamed x26, local copies, waits for them, and re-layouts  23.4 us
    all_to_all x1, starting transfers between devices, on_device(): lax.all_to_all(where_buf, 'seq', split_axis=0, concat_axis=0, tiled=True)  19.1 us
    gather x2, local copies, waits for them, and re-layouts, on_device(): numer_s.reshape(slot_total, heads_dev, head_dim)[slot_of, head_cols]  18.3 us
  transfers between devices with their start and end apart: 8, of which 6 were waited for; matrix products, arithmetic and copies ran while one was open for 11% of the time, Pallas kernels for 0%

commit v1 on v0

--- a/solution.py
+++ b/solution.py
@@ -69,7 +69,9 @@
     )
     where_buf = where_buf.reshape(owners, per_owner, MOST, heads_dev)
     cent_all_k, cent_all_v = (
-        lax.all_gather(cent_keys, "seq", axis=1, tiled=True),
+        jnp.concatenate(
+            lax.all_to_all(jnp.stack([cent_keys] * lax.axis_size("seq")), "seq", 0, 0), axis=1
+        ),
         lax.all_gather(cent_values, "seq", axis=1, tiled=True),
     )
     query_in = lax.all_to_all(place(queries), "seq", split_axis=0, concat_axis=0, tiled=True)

time: 808 us -> 612 us (0.76)
  blocking collectives: 453 us -> 234 us
  starting transfers between devices: 75.7 us -> 90.2 us
    all_gather x1 -> x0, blocking collectives: 225 us -> none  [on_device(): lax.all_gather(cent_keys, 'seq', axis=1, tiled=True)]
    unnamed x26 -> x23, local copies, waits for them, and re-layouts: 23.4 us -> 17.7 us
  transfers between devices with their start and end apart: 8 -> 9, of which waited for: 6 -> 7; matrix products, arithmetic and copies ran while one was open for 11% -> 17% of each run, Pallas kernels for 0% -> 0%
where the time goes in v1:
time: 612 us; the launch traced here: 610 us
  blocking collectives  234 us (38%)
  waiting for transfers between devices  132 us (22%)
  local copies, waits for them, and re-layouts  91.7 us (15%)
  starting transfers between devices  90.2 us (15%)
  other arithmetic  25 us (4%)
  matrix products  23.9 us (4%)
  between operations  13.8 us (2%)
    all_gather x1, blocking collectives, on_device(): lax.all_gather(cent_values, 'seq', axis=1, tiled=True)  234 us
    reduce_scatter x1, waiting for transfers between devices, on_device(): lax.psum_scatter(jnp.einsum('kc,tk->ct', out_weight, flat_out, preferred_...  60.3 us
    all_to_all x1, waiting for transfers between devices, on_device(): lax.all_to_all(place(queries), 'seq', split_axis=0, concat_axis=0, tiled=...  25.8 us
    all_to_all x1, waiting for transfers between devices, on_device(): lax.all_to_all(place(keys), 'seq', split_axis=0, concat_axis=0, tiled=True)  24.8 us
    all_to_all x1, starting transfers between devices, on_device(): lax.all_to_all(where_buf, 'seq', split_axis=0, concat_axis=0, tiled=True)  19.1 us
    gather x2, local copies, waits for them, and re-layouts, on_device(): numer_s.reshape(slot_total, heads_dev, head_dim)[slot_of, head_cols]  18.3 us
    unnamed x23, local copies, waits for them, and re-layouts  17.7 us
    all_to_all x1, starting transfers between devices, on_device(): lax.all_to_all(to_slots(denom, sources, depth).astype(jnp.bfloat16), 'seq...  15.1 us
  transfers between devices with their start and end apart: 9, of which 7 were waited for; matrix products, arithmetic and copies ran while one was open for 17% of the time, Pallas kernels for 0%

profile of v1, /device:TPU:2, one launch (start us, length us, event | category | flops | bytes accessed | tf_op | source)
XLA Modules:
  0.0 610.2 jit_solution(8008699133833834012)
XLA Ops:
  6.6 0.8 copy.185
  7.4 0.7 convert_reduce_fusion
  8.2 0.7 shift-left_or_fusion
  8.9 0.7 and_reduce_fusion
  9.6 0.8 multiply_reduce_fusion.1
  10.4 0.1 copy.121
  10.5 0.2 reshape.195
  10.9 0.2 reshape.197
  11.0 4.3 scatter_custom_fusion
  15.4 0.4 reshape.136
  15.8 0.7 copy.122
  16.5 19.1 %all-to-all-start = ((s32[64,4,8,2]{2,1,3,0:T(4,128)}), s32[64,4,8,2]{2,1,3,0:T(4,128)S(1)}, u32[]{:S(2)}, u32[]{:S(2)}) async-start(s32[64,4,8,2]{2,1,3,0:T(4,128)} %copy.122), calls=%async_computation | async-start | bytes 524288 | tf_op jit(solution)/shard_map/all_to_all | solution.py:80
  35.6 0.1 copy.125
  35.8 0.2 reshape.201
  35.9 3.9 scatter_custom_fusion.1
  39.8 1.2 reshape.137
  41.1 10.4 %all-to-all-done = s32[64,4,8,2]{2,1,3,0:T(4,128)S(1)} async-done(((s32[64,4,8,2]{2,1,3,0:T(4,128)}), s32[64,4,8,2]{2,1,3,0:T(4,128)S(1)}, u32[]{:S(2)}, u32[]{:S(2)}) %all-to-all-start) | async-done | bytes 16416 | tf_op jit(solution)/shard_map/all_to_all | solution.py:80
  51.5 6.4 %all-to-all-start.1 = ((bf16[64,4,8,256]{3,2,1,0:T(8,128)(2,1)}), bf16[64,4,8,256]{3,2,1,0:T(8,128)(2,1)}, u32[]{:S(2)}, u32[]{:S(2)}) async-start(bf16[64,4,8,256]{3,2,1,0:T(8,128)(2,1)} %reshape.137), calls=%async_computation.1 | async-start | bytes 2097152 | tf_op jit(solution)/shard_map/all_to_all | solution.py:77
  57.9 3.9 scatter_custom_fusion.2
  61.8 1.2 reshape.139
  63.0 25.8 %all-to-all-done.1 = bf16[64,4,8,256]{3,2,1,0:T(8,128)(2,1)} async-done(((bf16[64,4,8,256]{3,2,1,0:T(8,128)(2,1)}), bf16[64,4,8,256]{3,2,1,0:T(8,128)(2,1)}, u32[]{:S(2)}, u32[]{:S(2)}) %all-to-all-start.1) | async-done | bytes 1048608 | tf_op jit(solution)/shard_map/all_to_all | solution.py:77
  88.8 7.1 %all-to-all-start.2 = ((bf16[64,4,8,256]{3,2,1,0:T(8,128)(2,1)}), bf16[64,4,8,256]{3,2,1,0:T(8,128)(2,1)}, u32[]{:S(2)}, u32[]{:S(2)}) async-start(bf16[64,4,8,256]{3,2,1,0:T(8,128)(2,1)} %reshape.139), calls=%async_computation.2 | async-start | bytes 2097152 | tf_op jit(solution)/shard_map/all_to_all | solution.py:78
  95.9 4.1 scatter_custom_fusion.3
  100.0 1.2 reshape.141
  101.2 0.2 le.25
  101.5 24.8 %all-to-all-done.2 = bf16[64,4,8,256]{3,2,1,0:T(8,128)(2,1)} async-done(((bf16[64,4,8,256]{3,2,1,0:T(8,128)(2,1)}), bf16[64,4,8,256]{3,2,1,0:T(8,128)(2,1)}, u32[]{:S(2)}, u32[]{:S(2)}) %all-to-all-start.2) | async-done | bytes 1048608 | tf_op jit(solution)/shard_map/all_to_all | solution.py:78
  126.3 0.7 stack.2
  127.0 7.0 %all-to-all-start.6 = ((bf16[64,2,4,128]{3,2,1,0:T(4,128)(2,1)}), bf16[64,2,4,128]{3,2,1,0:T(4,128)(2,1)S(1)}, u32[]{:S(2)}, u32[]{:S(2)}) async-start(bf16[64,2,4,128]{3,2,1,0:T(4,128)(2,1)} %stack.2), calls=%async_computation.6 | async-start | bytes 262144 | tf_op jit(solution)/shard_map/all_to_all | solution.py:73
  134.1 13.3 %fusion = (f32[4,2,64,8]{3,2,1,0:T(8,128)S(1)}, f32[4,2,64,8,64,8]{4,3,5,2,1,0:T(8,128)}) fusion(s32[4,2,64,8]{3,2,1,0:T(8,128)S(1)} %bitcast.89, s32[4,2,64,8]{2,3,1,0:T(8,128)S(1)} %bitcast.92, pred[4,2,64,8]{2,3,1,0:T(8,128)(4,1)S(1)} %broadcast_compare_fusion, bf16[64,4,8,2,128,1]{4,2,3,1,0,5:T(8,128)(2,1)} %bitcast.10, ...), kind=kOutput, calls=%fused_computation.10 | convolution fusion | flops 547352576 | bytes 10539008 | tf_op jit(solution)/shard_map/aimhe,bikhe->ihambk/dot_general | solution.py:16
  147.4 0.6 all-to-all-done.6
  148.0 14.7 %all-to-all-start.3 = ((bf16[64,4,8,256]{3,2,1,0:T(8,128)(2,1)}), bf16[64,4,8,256]{3,2,1,0:T(8,128)(2,1)}, u32[]{:S(2)}, u32[]{:S(2)}) async-start(bf16[64,4,8,256]{3,2,1,0:T(8,128)(2,1)} %reshape.141), calls=%async_computation.3 | async-start | bytes 2097152 | tf_op jit(solution)/shard_map/all_to_all | solution.py:79
  162.7 9.2 %exponential_reduce_fusion = bf16[4,2,64,8]{3,2,1,0:T(8,128)(2,1)S(1)} fusion(f32[4,2,64,8,64,8]{4,3,5,2,1,0:T(8,128)} %get-tuple-element.14, f32[4,2,64,8]{3,2,1,0:T(8,128)S(1)} %get-tuple-element.13, s32[4,2,64,8]{3,2,1,0:T(8,128)S(1)} %bitcast.90, s32[4,2,64,8]{2,3,1,0:T(8,128)S(1)} %bitcast.93, pred[4,2,64,8]{2,3,1,0:T(8,128)(4,1)S(1)} %broadcast_compare_fusion), kind=kLoop, calls=%fused_computation.7 | loop fusion | flops 10481664 | bytes 8450048 | tf_op jit(solution)/shard_map/reduce_sum | solution.py:86
  171.9 0.2 sub.34
  172.1 9.4 %copy.128 = f32[4,2,64,8,64,8]{4,5,3,2,1,0:T(8,128)S(1)} copy(f32[4,2,64,8,64,8]{4,3,5,2,1,0:T(8,128)} %get-tuple-element.14) | data formatting | bytes 16777216 | tf_op jit(solution)/shard_map/mul | solution.py:19
  181.5 0.8 copy.145
  182.3 12.5 %exponential_convert_fusion = bf16[4,2,512,64,8]{3,4,2,1,0:T(8,128)(2,1)} fusion(f32[4,2,512,64,8]{3,4,2,1,0:T(8,128)S(1)} %bitcast.87, f32[4,2,512]{2,1,0:T(2,128)S(1)} %sub.34, s32[4,2,512]{2,1,0:T(2,128)S(1)} %le.25, s32[4,2,64,8]{2,3,1,0:T(8,128)S(1)} %bitcast.94, pred[4,2,64,8]{2,3,1,0:T(8,128)(4,1)S(1)} %broadcast_compare_fusion), kind=kLoop, calls=%fused_computation.8 | loop fusion | flops 10485760 | bytes 12636160 | tf_op jit(solution)/shard_map/convert_element_type | solution.py:85
  194.8 15.1 %all-to-all-start.7 = ((bf16[64,4,8,2]{2,1,3,0:T(4,128)(2,1)}), bf16[64,4,8,2]{2,1,3,0:T(4,128)(2,1)S(1)}, u32[]{:S(2)}, u32[]{:S(2)}) async-start(bf16[64,4,8,2]{2,1,3,0:T(4,128)(2,1)} %copy.145), calls=%async_computation.7 | async-start | bytes 262144 | tf_op jit(solution)/shard_map/all_to_all | solution.py:102
  209.9 0.8 copy.134
  210.7 12.0 %copy.130 = bf16[4,2,512,64,8]{2,4,3,1,0:T(8,128)(2,1)} copy(bf16[4,2,512,64,8]{3,4,2,1,0:T(8,128)(2,1)} %exponential_convert_fusion) | data formatting | bytes 8388608 | tf_op jit(solution)/shard_map/convert_element_type | solution.py:85
  222.7 1.0 all-to-all-done.7
  223.7 14.1 %all-to-all-start.5 = ((bf16[64,4,8,2]{2,1,3,0:T(4,128)(2,1)}), bf16[64,4,8,2]{2,1,3,0:T(4,128)(2,1)S(1)}, u32[]{:S(2)}, u32[]{:S(2)}) async-start(bf16[64,4,8,2]{2,1,3,0:T(4,128)(2,1)} %copy.134), calls=%async_computation.5 | async-start | bytes 262144 | tf_op jit(solution)/shard_map/all_to_all | solution.py:95
  237.8 4.0 fusion.2
  241.8 1.3 copy.183
  243.1 8.6 %all-to-all-done.5 = bf16[64,4,8,2]{2,1,3,0:T(4,128)(2,1)S(1)} async-done(((bf16[64,4,8,2]{2,1,3,0:T(4,128)(2,1)}), bf16[64,4,8,2]{2,1,3,0:T(4,128)(2,1)S(1)}, u32[]{:S(2)}, u32[]{:S(2)}) %all-to-all-start.5) | async-done | bytes 8224 | tf_op jit(solution)/shard_map/all_to_all | solution.py:95
  251.7 6.7 %all-to-all-start.4 = ((bf16[64,4,8,256]{3,2,1,0:T(8,128)(2,1)}), bf16[64,4,8,256]{3,2,1,0:T(8,128)(2,1)}, u32[]{:S(2)}, u32[]{:S(2)}) async-start(bf16[64,4,8,256]{3,2,1,0:T(8,128)(2,1)} %bitcast.84), calls=%async_computation.4 | async-start | bytes 2097152 | tf_op jit(solution)/shard_map/all_to_all | solution.py:88
  258.5 0.1 copy.133
  258.6 0.2 reshape.177
  258.8 234.0 %all_gather.3 = bf16[2,256,128]{2,0,1:T(2,128)(2,1)} all-gather(bf16[2,4,128]{2,0,1:T(2,128)(2,1)S(1)} %copy.142), channel_id=1, replica_groups=mesh['seq'=64,'head'=8] {'seq'}, dimensions={1}, use_global_device_ids=true | all-gather | bytes 133120 | tf_op jit(solution)/shard_map/all_gather | solution.py:75
  492.9 1.9 fusion.26
  495.0 0.3 reshape.176
  495.3 9.1 %gather_fusion.2 = f32[1024]{0:T(1024)S(1)} fusion(f32[2048,2]{0,1:T(2,128)S(1)} %reshape.176, s32[1024]{0:T(1024)S(1)} %reshape.177), kind=kCustom, calls=%fused_computation.2 | custom fusion | bytes 16384 | tf_op jit(solution)/shard_map/gather | solution.py:113
  504.4 0.2 reshape.192
  504.7 0.1 copy.135
  505.0 0.3 reshape.174
  505.3 9.1 %gather_fusion.1 = f32[1024]{0:T(1024)S(1)} fusion(f32[2048,2]{0,1:T(2,128)S(1)} %reshape.174, s32[1024]{0:T(1024)S(1)} %reshape.177), kind=kCustom, calls=%fused_computation.1 | custom fusion | bytes 16384 | tf_op jit(solution)/shard_map/gather | solution.py:112
  514.4 0.2 reshape.186
  514.7 0.2 fusion.10
  514.9 3.1 reshape.172
  518.0 16.2 %gather_fusion = f32[1024,128]{1,0:T(8,128)} fusion(f32[2048,2,128]{2,1,0:T(2,128)} %reshape.172, s32[1024]{0:T(1024)S(1)} %reshape.177), kind=kCustom, calls=%fused_computation | custom fusion | bytes 1056768 | tf_op jit(solution)/shard_map/gather | solution.py:111
  534.2 2.0 copy.141
  536.3 1.4 fusion.6
  537.7 3.2 fusion.1
  541.0 60.3 %reduce-scatter.2.cloned.1.call-done = bf16[512,512]{0,1:T(8,128)(2,1)} async-done(((bf16[4096,512]{0,1:T(8,128)(2,1)}), bf16[512,512]{0,1:T(8,128)(2,1)}) %reduce-scatter.2.cloned.1.call-update) | async-done | bytes 524304 | tf_op jit(solution)/shard_map/reduce_scatter | solution.py:129
  601.3 2.0 copy.149
  (35 shorter events, 1.2 us)
Async XLA Ops:
  6.5 531.2 %copy-start = (bf16[256,4096]{1,0:T(8,128)(2,1)S(1)}, bf16[256,4096]{1,0:T(8,128)(2,1)}, u32[]{:S(2)}) copy-start(bf16[256,4096]{1,0:T(8,128)(2,1)} %param.13) | copy-start | bytes 6291460
  11.0 115.3 %copy-start.4 = (bf16[2,4,128]{2,1,0:T(4,128)(2,1)S(1)}, bf16[2,4,128]{2,1,0:T(4,128)(2,1)}, u32[]{:S(2)}) copy-start(bf16[2,4,128]{2,1,0:T(4,128)(2,1)} %param.11) | copy-start | bytes 6148
  16.5 35.0 %all-to-all-start = ((s32[64,4,8,2]{2,1,3,0:T(4,128)}), s32[64,4,8,2]{2,1,3,0:T(4,128)S(1)}, u32[]{:S(2)}, u32[]{:S(2)}) async-start(s32[64,4,8,2]{2,1,3,0:T(4,128)} %copy.122), calls=%async_computation | async-start | bytes 524288 | tf_op jit(solution)/shard_map/all_to_all | solution.py:80
  51.5 37.3 %all-to-all-start.1 = ((bf16[64,4,8,256]{3,2,1,0:T(8,128)(2,1)}), bf16[64,4,8,256]{3,2,1,0:T(8,128)(2,1)}, u32[]{:S(2)}, u32[]{:S(2)}) async-start(bf16[64,4,8,256]{3,2,1,0:T(8,128)(2,1)} %reshape.137), calls=%async_computation.1 | async-start | bytes 2097152 | tf_op jit(solution)/shard_map/all_to_all | solution.py:77
  88.8 37.6 %all-to-all-start.2 = ((bf16[64,4,8,256]{3,2,1,0:T(8,128)(2,1)}), bf16[64,4,8,256]{3,2,1,0:T(8,128)(2,1)}, u32[]{:S(2)}, u32[]{:S(2)}) async-start(bf16[64,4,8,256]{3,2,1,0:T(8,128)(2,1)} %reshape.139), calls=%async_computation.2 | async-start | bytes 2097152 | tf_op jit(solution)/shard_map/all_to_all | solution.py:78
  127.0 20.9 %all-to-all-start.6 = ((bf16[64,2,4,128]{3,2,1,0:T(4,128)(2,1)}), bf16[64,2,4,128]{3,2,1,0:T(4,128)(2,1)S(1)}, u32[]{:S(2)}, u32[]{:S(2)}) async-start(bf16[64,2,4,128]{3,2,1,0:T(4,128)(2,1)} %stack.2), calls=%async_computation.6 | async-start | bytes 262144 | tf_op jit(solution)/shard_map/all_to_all | solution.py:73
  148.0 46.8 %all-to-all-start.3 = ((bf16[64,4,8,256]{3,2,1,0:T(8,128)(2,1)}), bf16[64,4,8,256]{3,2,1,0:T(8,128)(2,1)}, u32[]{:S(2)}, u32[]{:S(2)}) async-start(bf16[64,4,8,256]{3,2,1,0:T(8,128)(2,1)} %reshape.141), calls=%async_computation.3 | async-start | bytes 2097152 | tf_op jit(solution)/shard_map/all_to_all | solution.py:79
  194.8 28.9 %all-to-all-start.7 = ((bf16[64,4,8,2]{2,1,3,0:T(4,128)(2,1)}), bf16[64,4,8,2]{2,1,3,0:T(4,128)(2,1)S(1)}, u32[]{:S(2)}, u32[]{:S(2)}) async-start(bf16[64,4,8,2]{2,1,3,0:T(4,128)(2,1)} %copy.145), calls=%async_computation.7 | async-start | bytes 262144 | tf_op jit(solution)/shard_map/all_to_all | solution.py:102
  223.7 28.0 %all-to-all-start.5 = ((bf16[64,4,8,2]{2,1,3,0:T(4,128)(2,1)}), bf16[64,4,8,2]{2,1,3,0:T(4,128)(2,1)S(1)}, u32[]{:S(2)}, u32[]{:S(2)}) async-start(bf16[64,4,8,2]{2,1,3,0:T(4,128)(2,1)} %copy.134), calls=%async_computation.5 | async-start | bytes 262144 | tf_op jit(solution)/shard_map/all_to_all | solution.py:95
  237.8 21.0 %copy-start.5 = (bf16[2,4,128]{2,1,0:T(4,128)(2,1)S(1)}, bf16[2,4,128]{2,1,0:T(4,128)(2,1)}, u32[]{:S(2)}) copy-start(bf16[2,4,128]{2,1,0:T(4,128)(2,1)} %param.12) | copy-start | bytes 6148
  237.8 255.0 %copy-start.2 = (bf16[512,2,128]{2,1,0:T(2,128)(2,1)S(1)}, bf16[512,2,128]{2,1,0:T(2,128)(2,1)}, u32[]{:S(2)}) copy-start(bf16[512,2,128]{2,1,0:T(2,128)(2,1)} %param.7) | copy-start | bytes 786436
  251.7 263.2 %all-to-all-start.4 = ((bf16[64,4,8,256]{3,2,1,0:T(8,128)(2,1)}), bf16[64,4,8,256]{3,2,1,0:T(8,128)(2,1)}, u32[]{:S(2)}, u32[]{:S(2)}) async-start(bf16[64,4,8,256]{3,2,1,0:T(8,128)(2,1)} %bitcast.84), calls=%async_computation.4 | async-start | bytes 2097152 | tf_op jit(solution)/shard_map/all_to_all | solution.py:88
  258.4 342.9 %reduce-scatter.2.cloned.1.call-start = ((), (), s32[]{:S(2)}) async-start(), calls=%async_computation.9 | async-start | bytes 4718592 | tf_op jit(solution)/shard_map/reduce_scatter | solution.py:129
  505.3 9.4 %copy-start.3 = (f32[512,2]{0,1:T(2,128)S(1)}, f32[512,2]{0,1:T(2,128)}, u32[]{:S(2)}) copy-start(f32[512,2]{0,1:T(2,128)} %get-tuple-element.15) | copy-start | bytes 12292
  505.3 9.4 %copy-start.1 = (f32[512,2,256]{0,2,1:T(8,128)S(1)}, f32[512,2,256]{0,2,1:T(8,128)}, u32[]{:S(2)}) copy-start(f32[512,2,256]{0,2,1:T(8,128)} %get-tuple-element.16) | copy-start | bytes 3145732
Sparse Core Ops, SparseCore 0:
  541.1 60.1 reduce-scatter.1
